TPU v7x, 128 devices: a whole 4x4x4 slice. The times are simulated.
128 devices in a mesh: term: 4 (over x_hi, core), sec: 32 (over x_lo, z, y).
Axes of the slice: x: 4 (x_hi: 2, x_lo: 2; x = x_hi * 2 + x_lo), y: 4, z: 4, core: 2. Of those that a mesh axis runs over, the one named last changes fastest.
Arguments:
- psi_tiles: bfloat16 [768, 512, 512], P('sec'), may hold values from -6 to 6
- sectors: int32 [768, 2], P('sec'), may hold values from 0 to 15
- sources: int32 [4, 768], P('term', 'sec'), may hold values from 0 to 767, as said below
- left_env: bfloat16 [4, 16, 512, 512], P('term', None, 'sec'), may hold values from -0.25 to 0.25
- right_env: bfloat16 [4, 16, 512, 512], P('term', None, 'sec'), may hold values from -0.25 to 0.25
Outputs:
- applied: bfloat16 [768, 512, 512], P('sec', 'term')
Inputs may be any that keep to these rules, and one draw needn't show every extreme that they name: sources[t, k] lies in the same aligned block of 24 tiles as k, and each row maps each such block one to one onto itself.
All inputs are finite; a program needn't handle non-finite values.
Results may differ from a plain program's by a relative error of at most 0.013.
Values may be sent and summed in bfloat16 or wider, within the bound.
No kernel may reach another device: no remote copies, remote signals or barrier semaphores. Data moves between devices by JAX's collectives and lax.ppermute only.
A program may use at most 192 MiB of HBM per device.

v0:
```python
import jax
import jax.numpy as jnp
from jax import lax
from jax.sharding import PartitionSpec as P


def body(psi_tiles, sectors, sources, left_env, right_env):
    tile_count = psi_tiles.shape[0]
    width = psi_tiles.shape[2]
    local_ids = sources[0] - lax.axis_index("sec") * tile_count
    moved = jnp.take(psi_tiles, local_ids, axis=0)
    left_ids = sectors[:, 0]
    right_ids = sectors[:, 1]
    chosen = jnp.take(lax.all_gather(right_env[0], "sec", axis=1, tiled=True), right_ids, axis=0)
    half = jnp.einsum("kij,kjl->kil", moved, chosen, preferred_element_type=jnp.float32).astype(
        jnp.bfloat16
    )
    chosen = jnp.take(lax.all_gather(left_env[0], "sec", axis=1, tiled=True), left_ids, axis=0)
    term_out = jnp.einsum("kij,kjl->kil", chosen, half, preferred_element_type=jnp.float32)
    share_rows = width // lax.axis_size("term")
    summed = lax.psum(term_out.astype(jnp.bfloat16), "term").astype(jnp.float32)
    kept = lax.dynamic_slice_in_dim(summed, lax.axis_index("term") * share_rows, share_rows, 1)
    return kept.astype(jnp.bfloat16)


def solution(mesh):
    placed = (
        P("sec", None, None),
        P("sec", None),
        P("term", "sec"),
        P("term", None, "sec", None),
        P("term", None, "sec", None),
    )
    return jax.shard_map(
        body, mesh=mesh, in_specs=placed, out_specs=P("sec", "term", None), check_vma=False
    )
```

profile of v0, /device:TPU:1, one launch (start us, length us, event | category | flops | bytes accessed | tf_op | source)
XLA Modules:
  0.0 617.2 jit_solution(6412177317776371115)
XLA Ops:
  6.5 0.0 all-gather.7.cloned.1.call-start
  6.5 0.7 all-gather.7.cloned.1.call-update
  7.3 0.0 all-gather.5.cloned.1.call-start
  7.3 0.7 all-gather.5.cloned.1.call-update
  8.0 0.0 all-reduce.2.cloned.1.call-start
  8.1 0.7 fusion.30
  8.7 0.0 copy-start
  8.7 0.0 copy-start.1
  8.7 10.6 %gather_fusion = bf16[24,512,512]{2,1,0:T(8,128)(2,1)} fusion(bf16[24,512,512]{2,1,0:T(8,128)(2,1)} %param.7, s32[1024]{0:T(1024)S(1)} %pad_clamp_fusion.1), kind=kCustom, calls=%fused_computation.2 | custom fusion | bytes 25165920 | tf_op jit(solution)/shard_map/jit(_take)/gather | solution.py:11
  19.4 0.0 copy-done
  19.4 0.0 copy-done.1
  19.4 138.6 %all-gather.7.cloned.1.call-done = bf16[1,16,512,512]{3,2,1,0:T(8,128)(2,1)} async-done(((bf16[1,16,16,512]{3,2,1,0:T(8,128)(2,1)}), bf16[1,16,512,512]{3,2,1,0:T(8,128)(2,1)}) %all-gather.7.cloned.1.call-update) | async-done | bytes 8388624 | tf_op jit(solution)/shard_map/all_gather | solution.py:14
  158.0 9.5 %gather_fusion.2 = bf16[24,512,512]{2,1,0:T(8,128)(2,1)} fusion(bf16[16,512,512]{2,1,0:T(8,128)(2,1)} %bitcast.14, s32[1024]{0:T(1024)S(1)} %get-tuple-element.12), kind=kCustom, calls=%fused_computation.1.clone | custom fusion | bytes 25165920 | tf_op jit(solution)/shard_map/jit(_take)/gather | solution.py:14
  167.4 158.8 %all-gather.5.cloned.1.call-done = bf16[1,16,512,512]{3,2,1,0:T(8,128)(2,1)} async-done(((bf16[1,16,16,512]{3,2,1,0:T(8,128)(2,1)}), bf16[1,16,512,512]{3,2,1,0:T(8,128)(2,1)}) %all-gather.5.cloned.1.call-update) | async-done | bytes 8388624 | tf_op jit(solution)/shard_map/all_gather | solution.py:18
  326.3 9.5 %gather_fusion.1 = bf16[24,512,512]{2,1,0:T(8,128)(2,1)} fusion(bf16[16,512,512]{2,1,0:T(8,128)(2,1)} %bitcast.15, s32[1024]{0:T(1024)S(1)} %get-tuple-element.13), kind=kCustom, calls=%fused_computation.clone | custom fusion | bytes 25165920 | tf_op jit(solution)/shard_map/jit(_take)/gather | solution.py:18
  335.8 21.7 %fusion.19 = bf16[24,512,512]{2,1,0:T(8,128)(2,1)} fusion(bf16[24,512,512]{2,1,0:T(8,128)(2,1)} %gather_fusion.2, bf16[24,512,512]{2,1,0:T(8,128)(2,1)} %gather_fusion, pred[24]{0:T(512)(128)(4,1)S(1)} %get-tuple-element.10, pred[24]{0:T(512)(128)(4,1)S(1)} %compare_and_fusion.2, bf16[24,512,512]{2,1,0:T(8,128)(2,1)} %gather_fusion.1, ...), kind=kOutput, calls=%fused_computation.12 | convolution fusion | flops 12916359168 | bytes 50331720 | tf_op jit(solution)/shard_map/kij,kjl->kil/dot_general | solution.py:19
  357.5 0.0 all-reduce.2.cloned.1.call-update
  357.5 249.3 %all-reduce.2.cloned.1.call-done = bf16[24,512,512]{2,1,0:T(8,128)(2,1)} async-done(((bf16[24,512,512]{2,1,0:T(8,128)(2,1)}), bf16[24,512,512]{2,1,0:T(8,128)(2,1)}) %all-reduce.2.cloned.1.call-update) | async-done | bytes 12582928 | tf_op jit(solution)/shard_map/psum | solution.py:21
  606.8 3.9 convert_convert_fusion
  (4 shorter events, 0.0 us)
Async XLA Ops:
  6.5 151.4 %all-gather.7.cloned.1.call-start = ((), (), s32[]{:S(2)}) async-start(), calls=%async_computation.2 | async-start | bytes 8650752 | tf_op jit(solution)/shard_map/all_gather | solution.py:14
  7.3 319.0 %all-gather.5.cloned.1.call-start = ((), (), s32[]{:S(2)}) async-start(), calls=%async_computation.1 | async-start | bytes 8650752 | tf_op jit(solution)/shard_map/all_gather | solution.py:18
  8.0 598.8 %all-reduce.2.cloned.1.call-start = ((), (), s32[]{:S(2)}) async-start(), calls=%async_computation | async-start | bytes 25165824 | tf_op jit(solution)/shard_map/psum | solution.py:21
  8.7 10.6 %copy-start = (s32[24,2]{0,1:T(2,128)S(1)}, s32[24,2]{0,1:T(2,128)}, u32[]{:S(2)}) copy-start(s32[24,2]{0,1:T(2,128)} %param.8) | copy-start | bytes 580
  8.7 10.6 %copy-start.1 = (s32[1,24]{1,0:T(1,128)S(1)}, s32[1,24]{1,0:T(1,128)}, u32[]{:S(2)}) copy-start(s32[1,24]{1,0:T(1,128)} %param.9) | copy-start | bytes 292
Sparse Core Ops, SparseCore 0:
  9.0 148.9 all-gather.6
  159.6 166.6 all-gather.4
  357.6 249.1 all-reduce.1
where the time goes:
time: 617 us
  waiting for transfers between devices  548 us (89%)
  local copies, waits for them, and re-layouts  29.6 us (5%)
  matrix products  21.7 us (4%)
  between operations  13.2 us (2%)
    psum x1, waiting for transfers between devices, body(): summed = lax.psum(term_out.astype(jnp.bfloat16), 'term').astype(jnp.float32)  249 us
    all_gather x1, waiting for transfers between devices, body(): lax.all_gather(left_env[0], 'sec', axis=1, tiled=True)  159 us
    all_gather x1, waiting for transfers between devices, body(): lax.all_gather(right_env[0], 'sec', axis=1, tiled=True)  139 us
    dot_general x1, matrix products, body(): jnp.einsum('kij,kjl->kil', chosen, half, preferred_element_type=jnp.float32)  21.7 us
  transfers between devices with their start and end apart: 3, of which 3 were waited for; matrix products, arithmetic and copies ran while one was open for 3% of the time, Pallas kernels for 0%

commit v1 on v0

--- a/solution.py
+++ b/solution.py
@@ -18,7 +18,12 @@
     chosen = jnp.take(lax.all_gather(left_env[0], "sec", axis=1, tiled=True), left_ids, axis=0)
     term_out = jnp.einsum("kij,kjl->kil", chosen, half, preferred_element_type=jnp.float32)
     share_rows = width // lax.axis_size("term")
-    summed = lax.psum(term_out.astype(jnp.bfloat16), "term").astype(jnp.float32)
+
+    def read_digits_for(w_in, lane_axis):
+        current_arr = jax.lax.all_gather(w_in, axis_name=lane_axis)
+        return jnp.sum(current_arr, axis=0)
+
+    summed = read_digits_for(term_out.astype(jnp.bfloat16), "term").astype(jnp.float32)
     kept = lax.dynamic_slice_in_dim(summed, lax.axis_index("term") * share_rows, share_rows, 1)
     return kept.astype(jnp.bfloat16)
 

time: 617 us -> 714 us (1.16)
  waiting for transfers between devices: 548 us -> 621 us
  other arithmetic: 4.55 us -> 27.8 us
    all_gather x0 -> x1, waiting for transfers between devices: none -> 323 us  [read_digits_for(): current_arr = jax.lax.all_gather(w_in, axis_name=lane_axis)]
    psum x1 -> x0, waiting for transfers between devices: 249 us -> none  [body(): summed = lax.psum(term_out.astype(jnp.bfloat16), 'term').astype(jnp.float32)]
    reduce_sum x0 -> x1, other arithmetic: none -> 23.3 us  [read_digits_for(): return jnp.sum(current_arr, axis=0)]
where the time goes in v1:
time: 714 us
  waiting for transfers between devices  621 us (87%)
  local copies, waits for them, and re-layouts  29.6 us (4%)
  other arithmetic  27.8 us (4%)
  matrix products  21.7 us (3%)
  between operations  13.2 us (2%)
    all_gather x1, waiting for transfers between devices, read_digits_for(): current_arr = jax.lax.all_gather(w_in, axis_name=lane_axis)  323 us
    all_gather x1, waiting for transfers between devices, body(): lax.all_gather(left_env[0], 'sec', axis=1, tiled=True)  159 us
    all_gather x1, waiting for transfers between devices, body(): lax.all_gather(right_env[0], 'sec', axis=1, tiled=True)  139 us
    reduce_sum x1, other arithmetic, read_digits_for(): return jnp.sum(current_arr, axis=0)  23.3 us
    dot_general x1, matrix products, body(): jnp.einsum('kij,kjl->kil', chosen, half, preferred_element_type=jnp.float32)  21.7 us
  transfers between devices with their start and end apart: 3, of which 3 were waited for; matrix products, arithmetic and copies ran while one was open for 3% of the time, Pallas kernels for 0%

profile of v1, /device:TPU:1, one launch (start us, length us, event | category | flops | bytes accessed | tf_op | source)
XLA Modules:
  0.0 713.7 jit_solution(2164726085799862393)
XLA Ops:
  6.5 0.0 all-gather.9.cloned.1.call-start
  6.5 0.7 all-gather.9.cloned.1.call-update
  7.3 0.0 all-gather.7.cloned.1.call-start
  7.3 0.7 all-gather.7.cloned.1.call-update
  8.0 0.0 all-gather.11.cloned.1.call-start
  8.1 0.7 fusion.30
  8.7 0.0 copy-start
  8.7 0.0 copy-start.1
  8.7 10.6 %gather_fusion = bf16[24,512,512]{2,1,0:T(8,128)(2,1)} fusion(bf16[24,512,512]{2,1,0:T(8,128)(2,1)} %param.7, s32[1024]{0:T(1024)S(1)} %pad_clamp_fusion.1), kind=kCustom, calls=%fused_computation.2 | custom fusion | bytes 25165920 | tf_op jit(solution)/shard_map/jit(_take)/gather | solution.py:11
  19.4 0.0 copy-done
  19.4 0.0 copy-done.1
  19.4 138.6 %all-gather.9.cloned.1.call-done = bf16[1,16,512,512]{3,2,1,0:T(8,128)(2,1)} async-done(((bf16[1,16,16,512]{3,2,1,0:T(8,128)(2,1)}), bf16[1,16,512,512]{3,2,1,0:T(8,128)(2,1)}) %all-gather.9.cloned.1.call-update) | async-done | bytes 8388624 | tf_op jit(solution)/shard_map/all_gather | solution.py:14
  158.0 9.5 %gather_fusion.2 = bf16[24,512,512]{2,1,0:T(8,128)(2,1)} fusion(bf16[16,512,512]{2,1,0:T(8,128)(2,1)} %bitcast.16, s32[1024]{0:T(1024)S(1)} %get-tuple-element.12), kind=kCustom, calls=%fused_computation.1.clone | custom fusion | bytes 25165920 | tf_op jit(solution)/shard_map/jit(_take)/gather | solution.py:14
  167.4 158.8 %all-gather.7.cloned.1.call-done = bf16[1,16,512,512]{3,2,1,0:T(8,128)(2,1)} async-done(((bf16[1,16,16,512]{3,2,1,0:T(8,128)(2,1)}), bf16[1,16,512,512]{3,2,1,0:T(8,128)(2,1)}) %all-gather.7.cloned.1.call-update) | async-done | bytes 8388624 | tf_op jit(solution)/shard_map/all_gather | solution.py:18
  326.3 9.5 %gather_fusion.1 = bf16[24,512,512]{2,1,0:T(8,128)(2,1)} fusion(bf16[16,512,512]{2,1,0:T(8,128)(2,1)} %bitcast.17, s32[1024]{0:T(1024)S(1)} %get-tuple-element.13), kind=kCustom, calls=%fused_computation.clone | custom fusion | bytes 25165920 | tf_op jit(solution)/shard_map/jit(_take)/gather | solution.py:18
  335.8 21.7 %fusion.19 = bf16[24,512,512]{2,1,0:T(8,128)(2,1)} fusion(bf16[24,512,512]{2,1,0:T(8,128)(2,1)} %gather_fusion.2, bf16[24,512,512]{2,1,0:T(8,128)(2,1)} %gather_fusion, pred[24]{0:T(512)(128)(4,1)S(1)} %get-tuple-element.10, pred[24]{0:T(512)(128)(4,1)S(1)} %compare_and_fusion.2, bf16[24,512,512]{2,1,0:T(8,128)(2,1)} %gather_fusion.1, ...), kind=kOutput, calls=%fused_computation.12 | convolution fusion | flops 12916359168 | bytes 50331720 | tf_op jit(solution)/shard_map/kij,kjl->kil/dot_general | solution.py:19
  357.5 0.0 all-gather.11.cloned.1.call-update
  357.5 322.5 %all-gather.11.cloned.1.call-done = bf16[96,512,512]{2,1,0:T(8,128)(2,1)} async-done(((bf16[24,512,512]{2,1,0:T(8,128)(2,1)}), bf16[96,512,512]{2,1,0:T(8,128)(2,1)}) %all-gather.11.cloned.1.call-update) | async-done | bytes 50331664 | tf_op jit(solution)/shard_map/all_gather | solution.py:23
  680.0 23.3 %reduce_sum.12 = bf16[24,512,512]{2,1,0:T(8,128)(2,1)} reduce(bf16[4,24,512,512]{3,2,1,0:T(8,128)(2,1)} %bitcast.15, bf16[]{:T(256)} %constant.25.clone.1), dimensions={0}, to_apply=%region_0.0 | reduce | flops 18874368 | bytes 62914560 | tf_op jit(solution)/shard_map/reduce_sum | solution.py:24
  703.3 3.9 convert_convert_fusion
  (4 shorter events, 0.0 us)
Async XLA Ops:
  6.5 151.4 %all-gather.9.cloned.1.call-start = ((), (), s32[]{:S(2)}) async-start(), calls=%async_computation.1 | async-start | bytes 8650752 | tf_op jit(solution)/shard_map/all_gather | solution.py:14
  7.3 319.0 %all-gather.7.cloned.1.call-start = ((), (), s32[]{:S(2)}) async-start(), calls=%async_computation | async-start | bytes 8650752 | tf_op jit(solution)/shard_map/all_gather | solution.py:18
  8.0 672.0 %all-gather.11.cloned.1.call-start = ((), (), s32[]{:S(2)}) async-start(), calls=%async_computation.2 | async-start | bytes 62914560 | tf_op jit(solution)/shard_map/all_gather | solution.py:23
  8.7 10.6 %copy-start = (s32[24,2]{0,1:T(2,128)S(1)}, s32[24,2]{0,1:T(2,128)}, u32[]{:S(2)}) copy-start(s32[24,2]{0,1:T(2,128)} %param.8) | copy-start | bytes 580
  8.7 10.6 %copy-start.1 = (s32[1,24]{1,0:T(1,128)S(1)}, s32[1,24]{1,0:T(1,128)}, u32[]{:S(2)}) copy-start(s32[1,24]{1,0:T(1,128)} %param.9) | copy-start | bytes 292
Sparse Core Ops, SparseCore 0:
  9.0 148.9 all-gather.8
  159.6 166.6 all-gather.6
  357.6 322.3 all-gather.10
